TPU v7x, 32 devices: a whole 2x2x4 slice. The times are simulated.
32 devices in a mesh: section: 2 (over x), tm: 4 (over z), space: 4 (over y, core).
Axes of the slice: x: 2, y: 2, z: 4, core: 2. Of those that a mesh axis runs over, the one named last changes fastest.
Arguments:
- video: bfloat16 [2, 8, 16, 512, 128], P('section', 'tm', 'space'), may hold values from -6 to 6
- weights: bfloat16 [2, 9, 384, 128], P('section'), may hold values from -0.109375 to 0.109375
Outputs:
- decoded: bfloat16 [2, 8, 16, 512, 128], P('section', 'tm', 'space')
All inputs are finite; a program needn't handle non-finite values.
Results may differ from a plain program's by a relative error of at most 0.0095.
Values may be sent and summed in bfloat16 or wider, within the bound.
No kernel may reach another device: no remote copies, remote signals or barrier semaphores. Data moves between devices by JAX's collectives and lax.ppermute only.
A program may use at most 128 MiB of HBM per device.

v0:
```python
import jax
import jax.numpy as jnp
from jax import lax
from jax.sharding import PartitionSpec as P


def from_behind(block, axis, distance):
    devices = range(lax.axis_size(axis))
    route = [(i - distance, i) for i in devices if i - distance in devices]
    return lax.ppermute(block, axis, route)


def padded_2(cells, sides, width):
    for axis, dim in sides:
        count = lax.axis_size(axis)
        ends = count - 1
        head = lax.slice_in_dim(cells, 0, width, axis=dim)
        tail = lax.slice_in_dim(cells, cells.shape[dim] - width, cells.shape[dim], axis=dim)
        cells = jnp.concatenate(
            [
                lax.ppermute(tail, axis, [(i, (i + 1) % count) for i in range(ends)]),
                cells,
                lax.ppermute(head, axis, [((i + 1) % count, i) for i in range(ends)]),
            ],
            axis=dim,
        )
    return cells


def conv_block(clip, taps):
    frames, rows, width, chans = clip.shape
    act = jax.nn.silu(clip.astype(jnp.float32)).astype(jnp.bfloat16)
    carried = from_behind(act, "tm", 1)
    extended = jnp.concatenate([carried, act], axis=0)
    padded = padded_2(extended, (("space", 1),), 1)
    padded = jnp.pad(padded, ((0, 0), (0, 0), (1, 1), (0, 0)))
    joined = jnp.concatenate(
        [padded[:, :, 0:width], padded[:, :, 1 : width + 1], padded[:, :, 2 : width + 2]], axis=-1
    )
    total = jnp.zeros((frames * rows * width, chans), jnp.float32)
    for time_tap in range(3):
        for row_tap in range(3):
            slab = joined[time_tap : time_tap + frames, row_tap : row_tap + rows]
            total = total + jnp.dot(
                slab.reshape(-1, 3 * chans),
                taps[time_tap * 3 + row_tap],
                preferred_element_type=jnp.float32,
            )
    return (clip.astype(jnp.float32) + total.reshape(clip.shape)).astype(jnp.bfloat16)


def body(video, weights):
    all_taps = lax.all_gather(weights, "section", axis=0, tiled=True)
    first_taps = all_taps[0]
    second_taps = all_taps[1]
    index = 0
    hiddens = [conv_block(video[index], first_taps)]
    index = 0
    finished = [conv_block(hiddens[index], second_taps)]
    return jnp.stack(finished, axis=0)


def solution(mesh):
    return jax.shard_map(
        body,
        mesh=mesh,
        in_specs=(P("section", "tm", "space", None, None), P("section", None, None, None)),
        out_specs=P("section", "tm", "space", None, None),
        check_vma=False,
    )
```

profile of v0, /device:TPU:9, one launch (start us, length us, event | category | flops | bytes accessed | tf_op | source)
XLA Modules:
  0.0 177.2 jit_solution(865191045750303736)
XLA Ops:
  8.3 3.2 %collective-permute-start = (bf16[2,4,512,128]{3,2,1,0:T(8,128)(2,1)S(1)}, bf16[2,4,512,128]{3,2,1,0:T(8,128)(2,1)S(1)}, u32[]{:S(2)}, u32[]{:S(2)}) collective-permute-start(bf16[2,4,512,128]{3,2,1,0:T(8,128)(2,1)S(1)} %fusion.24), channel_id=1, source_target_pairs={{0,4},{4,8},{8,12},{1,5},{5,9},{9,13},{2,6},{6,10},{10,14},{3,7},{... | collective-permute-start | bytes 3145736 | tf_op jit(solution)/shard_map/ppermute | solution.py:10
  11.5 22.7 %collective-permute-done = bf16[2,4,512,128]{3,2,1,0:T(8,128)(2,1)S(1)} collective-permute-done((bf16[2,4,512,128]{3,2,1,0:T(8,128)(2,1)S(1)}, bf16[2,4,512,128]{3,2,1,0:T(8,128)(2,1)S(1)}, u32[]{:S(2)}, u32[]{:S(2)}) %collective-permute-start) | collective-permute-done | bytes 1048608 | tf_op jit(solution)/shard_map/ppermute | solution.py:10
  35.3 4.6 %collective-permute-start.1 = (bf16[4,1,512,128]{3,2,1,0:T(8,128)(2,1)}, bf16[4,1,512,128]{3,2,1,0:T(8,128)(2,1)S(1)}, u32[]{:S(2)}, u32[]{:S(2)}) collective-permute-start(bf16[4,1,512,128]{3,2,1,0:T(8,128)(2,1)} %get-tuple-element.29), channel_id=1, source_target_pairs={{0,1},{1,2},{2,3},{4,5},{5,6},{6,7},{8,9},{9,10},{10,11},{12,13},{... | collective-permute-start | bytes 1572872 | tf_op jit(solution)/shard_map/ppermute | solution.py:21
  41.8 4.5 %collective-permute-done.1 = bf16[4,1,512,128]{3,2,1,0:T(8,128)(2,1)S(1)} collective-permute-done((bf16[4,1,512,128]{3,2,1,0:T(8,128)(2,1)}, bf16[4,1,512,128]{3,2,1,0:T(8,128)(2,1)S(1)}, u32[]{:S(2)}, u32[]{:S(2)}) %collective-permute-start.1) | collective-permute-done | bytes 524320 | tf_op jit(solution)/shard_map/ppermute | solution.py:21
  46.3 4.3 %collective-permute-done.2 = bf16[4,1,512,128]{3,2,1,0:T(8,128)(2,1)S(1)} collective-permute-done((bf16[4,1,512,128]{3,2,1,0:T(8,128)(2,1)}, bf16[4,1,512,128]{3,2,1,0:T(8,128)(2,1)S(1)}, u32[]{:S(2)}, u32[]{:S(2)}) %collective-permute-start.2) | collective-permute-done | bytes 524320 | tf_op jit(solution)/shard_map/ppermute | solution.py:23
  52.5 2.3 %fusion.50 = (bf16[4,6,512,128]{3,2,1,0:T(8,128)(2,1)S(1)}, bf16[4,6,512,128]{3,2,1,0:T(8,128)(2,1)S(1)}) fusion(bf16[4,6,514,128]{3,2,1,0:T(8,128)(2,1)S(1)} %select_maximum_fusion.3), kind=kLoop, calls=%fused_computation.88 | loop fusion | bytes 12582912 | tf_op jit(solution)/shard_map/slice | solution.py:38
  56.5 9.3 %fusion.48 = (bf16[2,4,512,384]{3,2,1,0:T(8,128)(2,1)}, bf16[2,4,512,384]{3,2,1,0:T(8,128)(2,1)}, bf16[2,4,512,384]{3,2,1,0:T(8,128)(2,1)}, bf16[2,4,512,384]{3,...) fusion(bf16[4,6,512,384]{3,2,1,0:T(8,128)(2,1)S(1)} %pad_maximu, ...), kind=kLoop, calls=%fused_computation.86 | loop fusion | bytes 56623104 | tf_op jit(solution)/shard_map/slice | solution.py:43
  65.8 6.7 %all-gather.2.cloned.1.call-done = bf16[2,9,384,128]{3,2,1,0:T(8,128)(2,1)} async-done(((bf16[1,9,384,128]{3,2,1,0:T(8,128)(2,1)}), bf16[2,9,384,128]{3,2,1,0:T(8,128)(2,1)}) %all-gather.2.cloned.1.call-update) | async-done | bytes 1769488 | tf_op jit(solution)/shard_map/all_gather | solution.py:53
  72.5 3.0 %fusion.39 = f32[4096,128]{1,0:T(8,128)S(1)} fusion(bf16[4096,384]{1,0:T(8,128)(2,1)} %bitcast.128, bf16[2,9,384,128]{3,2,1,0:T(8,128)(2,1)} %all-gather.2.cloned.1.call-done), kind=kOutput, calls=%fused_computation.69 | convolution fusion | flops 402653184 | bytes 5341184 | tf_op jit(solution)/shard_map/dot_general | solution.py:44
  75.6 2.0 %fusion.40 = f32[4096,128]{1,0:T(8,128)S(1)} fusion(bf16[4096,384]{1,0:T(8,128)(2,1)S(1)} %bitcast.126, bf16[2,9,384,128]{3,2,1,0:T(8,128)(2,1)} %all-gather.2.cloned.1.call-done), kind=kOutput, calls=%fused_computation.71 | convolution fusion | flops 402653184 | bytes 5341184 | tf_op jit(solution)/shard_map/dot_general | solution.py:44
  77.6 2.0 %fusion.41 = f32[4096,128]{1,0:T(8,128)S(1)} fusion(bf16[4096,384]{1,0:T(8,128)(2,1)S(1)} %bitcast.124, bf16[2,9,384,128]{3,2,1,0:T(8,128)(2,1)} %all-gather.2.cloned.1.call-done), kind=kOutput, calls=%fused_computation.73 | convolution fusion | flops 402653184 | bytes 5341184 | tf_op jit(solution)/shard_map/dot_general | solution.py:44
  79.7 2.0 %fusion.42 = f32[4096,128]{1,0:T(8,128)S(1)} fusion(bf16[4096,384]{1,0:T(8,128)(2,1)S(1)} %bitcast.122, bf16[2,9,384,128]{3,2,1,0:T(8,128)(2,1)} %all-gather.2.cloned.1.call-done), kind=kOutput, calls=%fused_computation.75 | convolution fusion | flops 402653184 | bytes 5341184 | tf_op jit(solution)/shard_map/dot_general | solution.py:44
  81.7 2.0 %fusion.43 = f32[4096,128]{1,0:T(8,128)S(1)} fusion(bf16[4096,384]{1,0:T(8,128)(2,1)S(1)} %bitcast.120, bf16[2,9,384,128]{3,2,1,0:T(8,128)(2,1)} %all-gather.2.cloned.1.call-done), kind=kOutput, calls=%fused_computation.77 | convolution fusion | flops 402653184 | bytes 5341184 | tf_op jit(solution)/shard_map/dot_general | solution.py:44
  83.8 2.0 %fusion.44 = f32[4096,128]{1,0:T(8,128)S(1)} fusion(bf16[4096,384]{1,0:T(8,128)(2,1)S(1)} %bitcast.119, bf16[2,9,384,128]{3,2,1,0:T(8,128)(2,1)} %all-gather.2.cloned.1.call-done), kind=kOutput, calls=%fused_computation.79 | convolution fusion | flops 402653184 | bytes 5341184 | tf_op jit(solution)/shard_map/dot_general | solution.py:44
  87.7 2.0 %fusion.46 = f32[4096,128]{1,0:T(8,128)S(1)} fusion(bf16[4096,384]{1,0:T(8,128)(2,1)S(1)} %bitcast.117, bf16[2,9,384,128]{3,2,1,0:T(8,128)(2,1)} %all-gather.2.cloned.1.call-done), kind=kOutput, calls=%fused_computation.83 | convolution fusion | flops 402653184 | bytes 5341184 | tf_op jit(solution)/shard_map/dot_general | solution.py:44
  89.7 2.8 %fusion.14 = f32[4096,128]{1,0:T(8,128)S(1)} fusion(f32[4096,128]{1,0:T(8,128)S(1)} %fusion.39, f32[4096,128]{1,0:T(8,128)S(1)} %fusion.40, f32[4096,128]{1,0:T(8,128)S(1)} %fusion.41, f32[4096,128]{1,0:T(8,128)S(1)} %fusion.42, f32[4096,128]{1,0:T(8,128)S(1)} %fusion.43, f32[4096,128]{1,0:T(8,128)S(1)} %fusion.44, f32[4096,128]{1,0:T(8,128)S(1)} %fusion.45, ...), kind=kOutput, calls=%fused_computation.20 | convolution fusion | flops 406847488 | bytes 22118400 | tf_op jit(solution)/shard_map/dot_general | solution.py:44
  93.1 3.1 %collective-permute-start.3 = (bf16[2,4,512,128]{3,2,1,0:T(8,128)(2,1)S(1)}, bf16[2,4,512,128]{3,2,1,0:T(8,128)(2,1)S(1)}, u32[]{:S(2)}, u32[]{:S(2)}) collective-permute-start(bf16[2,4,512,128]{3,2,1,0:T(8,128)(2,1)S(1)} %fusion.30), channel_id=1, source_target_pairs={{0,4},{4,8},{8,12},{1,5},{5,9},{9,13},{2,6},{6,10},{10,14},{3,7},{... | collective-permute-start | bytes 3145736 | tf_op jit(solution)/shard_map/ppermute | solution.py:10
  96.3 22.8 %collective-permute-done.3 = bf16[2,4,512,128]{3,2,1,0:T(8,128)(2,1)S(1)} collective-permute-done((bf16[2,4,512,128]{3,2,1,0:T(8,128)(2,1)S(1)}, bf16[2,4,512,128]{3,2,1,0:T(8,128)(2,1)S(1)}, u32[]{:S(2)}, u32[]{:S(2)}) %collective-permute-start.3) | collective-permute-done | bytes 1048608 | tf_op jit(solution)/shard_map/ppermute | solution.py:10
  119.2 4.5 %collective-permute-start.4 = (bf16[4,1,512,128]{3,2,1,0:T(8,128)(2,1)S(1)}, bf16[4,1,512,128]{3,2,1,0:T(8,128)(2,1)S(1)}, u32[]{:S(2)}, u32[]{:S(2)}) collective-permute-start(bf16[4,1,512,128]{3,2,1,0:T(8,128)(2,1)S(1)} %get-tuple-element.27), channel_id=1, source_target_pairs={{0,1},{1,2},{2,3},{4,5},{5,6},{6,7},{8,9},{9,10},{10,11},{12,13},{... | collective-permute-start | bytes 1572872 | tf_op jit(solution)/shard_map/ppermute | solution.py:21
  123.7 1.9 %collective-permute-start.5 = (bf16[4,1,512,128]{3,2,1,0:T(8,128)(2,1)S(1)}, bf16[4,1,512,128]{3,2,1,0:T(8,128)(2,1)S(1)}, u32[]{:S(2)}, u32[]{:S(2)}) collective-permute-start(bf16[4,1,512,128]{3,2,1,0:T(8,128)(2,1)S(1)} %get-tuple-element.28), channel_id=1, source_target_pairs={{1,0},{2,1},{3,2},{5,4},{6,5},{7,6},{9,8},{10,9},{11,10},{13,12},{... | collective-permute-start | bytes 1572872 | tf_op jit(solution)/shard_map/ppermute | solution.py:23
  125.6 4.2 %collective-permute-done.4 = bf16[4,1,512,128]{3,2,1,0:T(8,128)(2,1)S(1)} collective-permute-done((bf16[4,1,512,128]{3,2,1,0:T(8,128)(2,1)S(1)}, bf16[4,1,512,128]{3,2,1,0:T(8,128)(2,1)S(1)}, u32[]{:S(2)}, u32[]{:S(2)}) %collective-permute-start.4) | collective-permute-done | bytes 524320 | tf_op jit(solution)/shard_map/ppermute | solution.py:21
  129.8 4.4 %collective-permute-done.5 = bf16[4,1,512,128]{3,2,1,0:T(8,128)(2,1)S(1)} collective-permute-done((bf16[4,1,512,128]{3,2,1,0:T(8,128)(2,1)S(1)}, bf16[4,1,512,128]{3,2,1,0:T(8,128)(2,1)S(1)}, u32[]{:S(2)}, u32[]{:S(2)}) %collective-permute-start.5) | collective-permute-done | bytes 524320 | tf_op jit(solution)/shard_map/ppermute | solution.py:23
  136.1 2.3 %fusion.49 = (bf16[4,6,512,128]{3,2,1,0:T(8,128)(2,1)S(1)}, bf16[4,6,512,128]{3,2,1,0:T(8,128)(2,1)S(1)}) fusion(bf16[4,6,514,128]{3,2,1,0:T(8,128)(2,1)S(1)} %select_maximum_fusion), kind=kLoop, calls=%fused_computation.87 | loop fusion | bytes 12582912 | tf_op jit(solution)/shard_map/slice | solution.py:38
  140.1 9.3 %fusion.47 = (bf16[2,4,512,384]{3,2,1,0:T(8,128)(2,1)}, bf16[2,4,512,384]{3,2,1,0:T(8,128)(2,1)}, bf16[2,4,512,384]{3,2,1,0:T(8,128)(2,1)}, bf16[2,4,512,384]{3,...) fusion(bf16[4,6,512,384]{3,2,1,0:T(8,128)(2,1)S(1)} %pad_maximu, ...), kind=kLoop, calls=%fused_computation.85 | loop fusion | bytes 56623104 | tf_op jit(solution)/shard_map/slice | solution.py:43
  149.5 3.0 %fusion.31 = f32[4096,128]{1,0:T(8,128)S(1)} fusion(bf16[4096,384]{1,0:T(8,128)(2,1)} %bitcast.132, bf16[2,9,384,128]{3,2,1,0:T(8,128)(2,1)} %all-gather.2.cloned.1.call-done), kind=kOutput, calls=%fused_computation.52 | convolution fusion | flops 402653184 | bytes 5341184 | tf_op jit(solution)/shard_map/dot_general | solution.py:44
  152.5 2.0 %fusion.32 = f32[4096,128]{1,0:T(8,128)S(1)} fusion(bf16[4096,384]{1,0:T(8,128)(2,1)S(1)} %bitcast.131, bf16[2,9,384,128]{3,2,1,0:T(8,128)(2,1)} %all-gather.2.cloned.1.call-done), kind=kOutput, calls=%fused_computation.54 | convolution fusion | flops 402653184 | bytes 5341184 | tf_op jit(solution)/shard_map/dot_general | solution.py:44
  154.6 2.0 %fusion.33 = f32[4096,128]{1,0:T(8,128)S(1)} fusion(bf16[4096,384]{1,0:T(8,128)(2,1)S(1)} %bitcast.130, bf16[2,9,384,128]{3,2,1,0:T(8,128)(2,1)} %all-gather.2.cloned.1.call-done), kind=kOutput, calls=%fused_computation.56 | convolution fusion | flops 402653184 | bytes 5341184 | tf_op jit(solution)/shard_map/dot_general | solution.py:44
  156.6 2.0 %fusion.34 = f32[4096,128]{1,0:T(8,128)S(1)} fusion(bf16[4096,384]{1,0:T(8,128)(2,1)S(1)} %bitcast.129, bf16[2,9,384,128]{3,2,1,0:T(8,128)(2,1)} %all-gather.2.cloned.1.call-done), kind=kOutput, calls=%fused_computation.58 | convolution fusion | flops 402653184 | bytes 5341184 | tf_op jit(solution)/shard_map/dot_general | solution.py:44
  158.7 2.0 %fusion.35 = f32[4096,128]{1,0:T(8,128)S(1)} fusion(bf16[4096,384]{1,0:T(8,128)(2,1)S(1)} %bitcast.127, bf16[2,9,384,128]{3,2,1,0:T(8,128)(2,1)} %all-gather.2.cloned.1.call-done), kind=kOutput, calls=%fused_computation.60 | convolution fusion | flops 402653184 | bytes 5341184 | tf_op jit(solution)/shard_map/dot_general | solution.py:44
  160.7 2.0 %fusion.36 = f32[4096,128]{1,0:T(8,128)S(1)} fusion(bf16[4096,384]{1,0:T(8,128)(2,1)S(1)} %bitcast.125, bf16[2,9,384,128]{3,2,1,0:T(8,128)(2,1)} %all-gather.2.cloned.1.call-done), kind=kOutput, calls=%fused_computation.62 | convolution fusion | flops 402653184 | bytes 5341184 | tf_op jit(solution)/shard_map/dot_general | solution.py:44
  164.6 2.0 %fusion.38 = f32[4096,128]{1,0:T(8,128)S(1)} fusion(bf16[4096,384]{1,0:T(8,128)(2,1)S(1)} %bitcast.121, bf16[2,9,384,128]{3,2,1,0:T(8,128)(2,1)} %all-gather.2.cloned.1.call-done), kind=kOutput, calls=%fused_computation.66 | convolution fusion | flops 402653184 | bytes 5341184 | tf_op jit(solution)/shard_map/dot_general | solution.py:44
  166.7 2.5 %fusion.11 = f32[4096,128]{1,0:T(8,128)S(1)} fusion(f32[4096,128]{1,0:T(8,128)S(1)} %fusion.31, f32[4096,128]{1,0:T(8,128)S(1)} %fusion.32, f32[4096,128]{1,0:T(8,128)S(1)} %fusion.33, f32[4096,128]{1,0:T(8,128)S(1)} %fusion.34, f32[4096,128]{1,0:T(8,128)S(1)} %fusion.35, f32[4096,128]{1,0:T(8,128)S(1)} %fusion.36, f32[4096,128]{1,0:T(8,128)S(1)} %fusion.37, ...), kind=kOutput, calls=%fused_computation.17 | convolution fusion | flops 406847488 | bytes 22118400 | tf_op jit(solution)/shard_map/dot_general | solution.py:44
  (44 shorter events, 17.7 us)
Async XLA Ops:
  6.5 66.0 %all-gather.2.cloned.1.call-start = ((), (), s32[]{:S(2)}) async-start(), calls=%async_computation | async-start | bytes 2654208 | tf_op jit(solution)/shard_map/all_gather | solution.py:53
  8.3 25.9 %collective-permute-start = (bf16[2,4,512,128]{3,2,1,0:T(8,128)(2,1)S(1)}, bf16[2,4,512,128]{3,2,1,0:T(8,128)(2,1)S(1)}, u32[]{:S(2)}, u32[]{:S(2)}) collective-permute-start(bf16[2,4,512,128]{3,2,1,0:T(8,128)(2,1)S(1)} %fusion.24), channel_id=1, source_target_pairs={{0,4},{4,8},{8,12},{1,5},{5,9},{9,13},{2,6},{6,10},{10,14},{3,7},{... | collective-permute-start | bytes 3145736 | tf_op jit(solution)/shard_map/ppermute | solution.py:10
  35.3 11.0 %collective-permute-start.1 = (bf16[4,1,512,128]{3,2,1,0:T(8,128)(2,1)}, bf16[4,1,512,128]{3,2,1,0:T(8,128)(2,1)S(1)}, u32[]{:S(2)}, u32[]{:S(2)}) collective-permute-start(bf16[4,1,512,128]{3,2,1,0:T(8,128)(2,1)} %get-tuple-element.29), channel_id=1, source_target_pairs={{0,1},{1,2},{2,3},{4,5},{5,6},{6,7},{8,9},{9,10},{10,11},{12,13},{... | collective-permute-start | bytes 1572872 | tf_op jit(solution)/shard_map/ppermute | solution.py:21
  39.9 10.7 %collective-permute-start.2 = (bf16[4,1,512,128]{3,2,1,0:T(8,128)(2,1)}, bf16[4,1,512,128]{3,2,1,0:T(8,128)(2,1)S(1)}, u32[]{:S(2)}, u32[]{:S(2)}) collective-permute-start(bf16[4,1,512,128]{3,2,1,0:T(8,128)(2,1)} %get-tuple-element.30), channel_id=1, source_target_pairs={{1,0},{2,1},{3,2},{5,4},{6,5},{7,6},{9,8},{10,9},{11,10},{13,12},{... | collective-permute-start | bytes 1572872 | tf_op jit(solution)/shard_map/ppermute | solution.py:23
  72.5 3.0 %copy-start.7 = (bf16[2,4,512,384]{3,2,1,0:T(8,128)(2,1)S(1)}, bf16[2,4,512,384]{3,2,1,0:T(8,128)(2,1)}, u32[]{:S(2)}) copy-start(bf16[2,4,512,384]{3,2,1,0:T(8,128)(2,1)} %get-tuple-element.16) | copy-start | bytes 9437188
  75.6 2.0 %copy-start.5 = (bf16[2,4,512,384]{3,2,1,0:T(8,128)(2,1)S(1)}, bf16[2,4,512,384]{3,2,1,0:T(8,128)(2,1)}, u32[]{:S(2)}) copy-start(bf16[2,4,512,384]{3,2,1,0:T(8,128)(2,1)} %get-tuple-element.17) | copy-start | bytes 9437188
  77.6 2.0 %copy-start.3 = (bf16[2,4,512,384]{3,2,1,0:T(8,128)(2,1)S(1)}, bf16[2,4,512,384]{3,2,1,0:T(8,128)(2,1)}, u32[]{:S(2)}) copy-start(bf16[2,4,512,384]{3,2,1,0:T(8,128)(2,1)} %get-tuple-element.18) | copy-start | bytes 9437188
  79.6 2.0 %copy-start.2 = (bf16[2,4,512,384]{3,2,1,0:T(8,128)(2,1)S(1)}, bf16[2,4,512,384]{3,2,1,0:T(8,128)(2,1)}, u32[]{:S(2)}) copy-start(bf16[2,4,512,384]{3,2,1,0:T(8,128)(2,1)} %get-tuple-element.19) | copy-start | bytes 9437188
  81.7 2.0 %copy-start.1 = (bf16[2,4,512,384]{3,2,1,0:T(8,128)(2,1)S(1)}, bf16[2,4,512,384]{3,2,1,0:T(8,128)(2,1)}, u32[]{:S(2)}) copy-start(bf16[2,4,512,384]{3,2,1,0:T(8,128)(2,1)} %get-tuple-element.20) | copy-start | bytes 9437188
  83.8 2.0 %copy-start = (bf16[2,4,512,384]{3,2,1,0:T(8,128)(2,1)S(1)}, bf16[2,4,512,384]{3,2,1,0:T(8,128)(2,1)}, u32[]{:S(2)}) copy-start(bf16[2,4,512,384]{3,2,1,0:T(8,128)(2,1)} %get-tuple-element.21) | copy-start | bytes 9437188
  87.7 2.0 %copy-start.12 = (bf16[2,4,512,384]{3,2,1,0:T(8,128)(2,1)S(1)}, bf16[2,4,512,384]{3,2,1,0:T(8,128)(2,1)}, u32[]{:S(2)}) copy-start(bf16[2,4,512,384]{3,2,1,0:T(8,128)(2,1)} %get-tuple-element.14) | copy-start | bytes 9437188
  89.7 2.8 %copy-start.14 = (bf16[1,2,4,512,128]{4,3,2,1,0:T(8,128)(2,1)S(1)}, bf16[1,2,4,512,128]{4,3,2,1,0:T(8,128)(2,1)}, u32[]{:S(2)}) copy-start(bf16[1,2,4,512,128]{4,3,2,1,0:T(8,128)(2,1)} %param.2) | copy-start | bytes 3145732
  93.1 25.9 %collective-permute-start.3 = (bf16[2,4,512,128]{3,2,1,0:T(8,128)(2,1)S(1)}, bf16[2,4,512,128]{3,2,1,0:T(8,128)(2,1)S(1)}, u32[]{:S(2)}, u32[]{:S(2)}) collective-permute-start(bf16[2,4,512,128]{3,2,1,0:T(8,128)(2,1)S(1)} %fusion.30), channel_id=1, source_target_pairs={{0,4},{4,8},{8,12},{1,5},{5,9},{9,13},{2,6},{6,10},{10,14},{3,7},{... | collective-permute-start | bytes 3145736 | tf_op jit(solution)/shard_map/ppermute | solution.py:10
  119.2 10.6 %collective-permute-start.4 = (bf16[4,1,512,128]{3,2,1,0:T(8,128)(2,1)S(1)}, bf16[4,1,512,128]{3,2,1,0:T(8,128)(2,1)S(1)}, u32[]{:S(2)}, u32[]{:S(2)}) collective-permute-start(bf16[4,1,512,128]{3,2,1,0:T(8,128)(2,1)S(1)} %get-tuple-element.27), channel_id=1, source_target_pairs={{0,1},{1,2},{2,3},{4,5},{5,6},{6,7},{8,9},{9,10},{10,11},{12,13},{... | collective-permute-start | bytes 1572872 | tf_op jit(solution)/shard_map/ppermute | solution.py:21
  123.7 10.5 %collective-permute-start.5 = (bf16[4,1,512,128]{3,2,1,0:T(8,128)(2,1)S(1)}, bf16[4,1,512,128]{3,2,1,0:T(8,128)(2,1)S(1)}, u32[]{:S(2)}, u32[]{:S(2)}) collective-permute-start(bf16[4,1,512,128]{3,2,1,0:T(8,128)(2,1)S(1)} %get-tuple-element.28), channel_id=1, source_target_pairs={{1,0},{2,1},{3,2},{5,4},{6,5},{7,6},{9,8},{10,9},{11,10},{13,12},{... | collective-permute-start | bytes 1572872 | tf_op jit(solution)/shard_map/ppermute | solution.py:23
  149.5 3.0 %copy-start.11 = (bf16[2,4,512,384]{3,2,1,0:T(8,128)(2,1)S(1)}, bf16[2,4,512,384]{3,2,1,0:T(8,128)(2,1)}, u32[]{:S(2)}) copy-start(bf16[2,4,512,384]{3,2,1,0:T(8,128)(2,1)} %get-tuple-element.7) | copy-start | bytes 9437188
  152.5 2.0 %copy-start.10 = (bf16[2,4,512,384]{3,2,1,0:T(8,128)(2,1)S(1)}, bf16[2,4,512,384]{3,2,1,0:T(8,128)(2,1)}, u32[]{:S(2)}) copy-start(bf16[2,4,512,384]{3,2,1,0:T(8,128)(2,1)} %get-tuple-element.8) | copy-start | bytes 9437188
  154.6 2.0 %copy-start.9 = (bf16[2,4,512,384]{3,2,1,0:T(8,128)(2,1)S(1)}, bf16[2,4,512,384]{3,2,1,0:T(8,128)(2,1)}, u32[]{:S(2)}) copy-start(bf16[2,4,512,384]{3,2,1,0:T(8,128)(2,1)} %get-tuple-element.9) | copy-start | bytes 9437188
  156.6 2.0 %copy-start.8 = (bf16[2,4,512,384]{3,2,1,0:T(8,128)(2,1)S(1)}, bf16[2,4,512,384]{3,2,1,0:T(8,128)(2,1)}, u32[]{:S(2)}) copy-start(bf16[2,4,512,384]{3,2,1,0:T(8,128)(2,1)} %get-tuple-element.10) | copy-start | bytes 9437188
  158.6 2.0 %copy-start.6 = (bf16[2,4,512,384]{3,2,1,0:T(8,128)(2,1)S(1)}, bf16[2,4,512,384]{3,2,1,0:T(8,128)(2,1)}, u32[]{:S(2)}) copy-start(bf16[2,4,512,384]{3,2,1,0:T(8,128)(2,1)} %get-tuple-element.11) | copy-start | bytes 9437188
  160.7 2.0 %copy-start.4 = (bf16[2,4,512,384]{3,2,1,0:T(8,128)(2,1)S(1)}, bf16[2,4,512,384]{3,2,1,0:T(8,128)(2,1)}, u32[]{:S(2)}) copy-start(bf16[2,4,512,384]{3,2,1,0:T(8,128)(2,1)} %get-tuple-element.12) | copy-start | bytes 9437188
  164.6 2.0 %copy-start.13 = (bf16[2,4,512,384]{3,2,1,0:T(8,128)(2,1)S(1)}, bf16[2,4,512,384]{3,2,1,0:T(8,128)(2,1)}, u32[]{:S(2)}) copy-start(bf16[2,4,512,384]{3,2,1,0:T(8,128)(2,1)} %get-tuple-element.5) | copy-start | bytes 9437188
Sparse Core Ops, SparseCore 0:
  42.0 30.5 all-gather.1
where the time goes:
time: 178 us; the launch traced here: 177 us
  waiting for transfers between devices  69.6 us (39%)
  matrix products  39.3 us (22%)
  local copies, waits for them, and re-layouts  23.3 us (13%)
  starting transfers between devices  19.2 us (11%)
  between operations  13.9 us (8%)
  other arithmetic  12 us (7%)
    ppermute x2, waiting for transfers between devices, from_behind(): return lax.ppermute(block, axis, route)  45.5 us
    dot_general x18, matrix products, conv_block(): jnp.dot(slab.reshape(-1, 3 * chans), taps[time_tap * 3 + row_tap], prefer...  39.3 us
    slice x2, local copies, waits for them, and re-layouts, conv_block(): slab = joined[time_tap:time_tap + frames, row_tap:row_tap + rows]  18.6 us
    ppermute x2, starting transfers between devices, padded_2(): lax.ppermute(tail, axis, [(i, (i + 1) % count) for i in range(ends)])  9.08 us
    ppermute x2, waiting for transfers between devices, padded_2(): lax.ppermute(head, axis, [((i + 1) % count, i) for i in range(ends)])  8.69 us
    ppermute x2, waiting for transfers between devices, padded_2(): lax.ppermute(tail, axis, [(i, (i + 1) % count) for i in range(ends)])  8.64 us
    all_gather x1, waiting for transfers between devices, body(): all_taps = lax.all_gather(weights, 'section', axis=0, tiled=True)  6.69 us
    ppermute x2, starting transfers between devices, from_behind(): return lax.ppermute(block, axis, route)  6.32 us
  transfers between devices with their start and end apart: 7, of which 7 were waited for; matrix products, arithmetic and copies ran while one was open for 9% of the time, Pallas kernels for 0%

commit v1 on v0

--- a/solution.py
+++ b/solution.py
@@ -2,6 +2,18 @@
 import jax.numpy as jnp
 from jax import lax
 from jax.sharding import PartitionSpec as P
+
+
+def collect(value, axis, dim):
+    ways, here = (lax.axis_size(axis), lax.axis_index(axis))
+    grown, reach = (value, 1)
+    while reach < ways:
+        theirs = lax.ppermute(grown, axis, [(d, d ^ reach) for d in range(ways)])
+        mine_first = jnp.concatenate([grown, theirs], axis=dim)
+        theirs_first = jnp.concatenate([theirs, grown], axis=dim)
+        grown = jnp.where(here & reach == 0, mine_first, theirs_first)
+        reach = 2 * reach
+    return grown
 
 
 def from_behind(block, axis, distance):
@@ -50,7 +62,7 @@
 
 
 def body(video, weights):
-    all_taps = lax.all_gather(weights, "section", axis=0, tiled=True)
+    all_taps = collect(weights, "section", 0)
     first_taps = all_taps[0]
     second_taps = all_taps[1]
     index = 0

time: 178 us -> 153 us (0.86)
  waiting for transfers between devices: 69.6 us -> 52.5 us
  between operations: 13.9 us -> 0.52 us
  other arithmetic: 12 us -> 17.9 us
    ppermute x2, waiting for transfers between devices: 45.5 us -> 38.8 us  [from_behind(): return lax.ppermute(block, axis, route)]
    all_gather x1 -> x0, waiting for transfers between devices: 6.69 us -> none  [body(): all_taps = lax.all_gather(weights, 'section', axis=0, tiled=True)]
    select_n x0 -> x1, other arithmetic: none -> 3.56 us  [collect(): grown = jnp.where(here & reach == 0, mine_first, theirs_first)]
    ppermute x2, waiting for transfers between devices: 8.64 us -> 5.09 us  [padded_2(): lax.ppermute(tail, axis, [(i, (i + 1) % count) for i in range(ends)])]
    concatenate x2, other arithmetic: 3.45 us -> 5.67 us  [conv_block(): jnp.concatenate([padded[:, :, 0:width], padded[:, :, 1:width + 1], padded...]
  transfers between devices with their start and end apart: 7 -> 7, of which waited for: 7 -> 6; matrix products, arithmetic and copies ran while one was open for 9% -> 3% of each run, Pallas kernels for 0% -> 0%
where the time goes in v1:
time: 153 us; the launch traced here: 152 us
  waiting for transfers between devices  52.5 us (34%)
  matrix products  38.9 us (25%)
  local copies, waits for them, and re-layouts  22.5 us (15%)
  starting transfers between devices  19.8 us (13%)
  other arithmetic  17.9 us (12%)
    dot_general x18, matrix products, conv_block(): jnp.dot(slab.reshape(-1, 3 * chans), taps[time_tap * 3 + row_tap], prefer...  38.9 us
    ppermute x2, waiting for transfers between devices, from_behind(): return lax.ppermute(block, axis, route)  38.8 us
    slice x2, local copies, waits for them, and re-layouts, conv_block(): slab = joined[time_tap:time_tap + frames, row_tap:row_tap + rows]  17.8 us
    ppermute x2, waiting for transfers between devices, padded_2(): lax.ppermute(head, axis, [((i + 1) % count, i) for i in range(ends)])  8.68 us
    ppermute x2, starting transfers between devices, padded_2(): lax.ppermute(tail, axis, [(i, (i + 1) % count) for i in range(ends)])  8.25 us
    ppermute x2, starting transfers between devices, from_behind(): return lax.ppermute(block, axis, route)  6.41 us
    concatenate x2, other arithmetic, conv_block(): jnp.concatenate([padded[:, :, 0:width], padded[:, :, 1:width + 1], padded...  5.67 us
    ppermute x2, waiting for transfers between devices, padded_2(): lax.ppermute(tail, axis, [(i, (i + 1) % count) for i in range(ends)])  5.09 us
  transfers between devices with their start and end apart: 7, of which 6 were waited for; matrix products, arithmetic and copies ran while one was open for 3% of the time, Pallas kernels for 0%

profile of v1, /device:TPU:9, one launch (start us, length us, event | category | flops | bytes accessed | tf_op | source)
XLA Modules:
  0.0 152.1 jit_solution(8554043182278701610)
XLA Ops:
  1.8 3.2 %collective-permute-start = (bf16[2,4,512,128]{3,2,1,0:T(8,128)(2,1)S(1)}, bf16[2,4,512,128]{3,2,1,0:T(8,128)(2,1)S(1)}, u32[]{:S(2)}, u32[]{:S(2)}) collective-permute-start(bf16[2,4,512,128]{3,2,1,0:T(8,128)(2,1)S(1)} %fusion.24), channel_id=1, source_target_pairs={{0,4},{4,8},{8,12},{1,5},{5,9},{9,13},{2,6},{6,10},{10,14},{3,7},{... | collective-permute-start | bytes 3145736 | tf_op jit(solution)/shard_map/ppermute | solution.py:22
  6.3 21.4 %collective-permute-done = bf16[2,4,512,128]{3,2,1,0:T(8,128)(2,1)S(1)} collective-permute-done((bf16[2,4,512,128]{3,2,1,0:T(8,128)(2,1)S(1)}, bf16[2,4,512,128]{3,2,1,0:T(8,128)(2,1)S(1)}, u32[]{:S(2)}, u32[]{:S(2)}) %collective-permute-start) | collective-permute-done | bytes 1048608 | tf_op jit(solution)/shard_map/ppermute | solution.py:22
  28.9 4.6 %collective-permute-start.1 = (bf16[4,1,512,128]{3,2,1,0:T(8,128)(2,1)}, bf16[4,1,512,128]{3,2,1,0:T(8,128)(2,1)S(1)}, u32[]{:S(2)}, u32[]{:S(2)}) collective-permute-start(bf16[4,1,512,128]{3,2,1,0:T(8,128)(2,1)} %get-tuple-element.29), channel_id=1, source_target_pairs={{0,1},{1,2},{2,3},{4,5},{5,6},{6,7},{8,9},{9,10},{10,11},{12,13},{... | collective-permute-start | bytes 1572872 | tf_op jit(solution)/shard_map/ppermute | solution.py:33
  33.5 1.9 %collective-permute-start.2 = (bf16[4,1,512,128]{3,2,1,0:T(8,128)(2,1)}, bf16[4,1,512,128]{3,2,1,0:T(8,128)(2,1)S(1)}, u32[]{:S(2)}, u32[]{:S(2)}) collective-permute-start(bf16[4,1,512,128]{3,2,1,0:T(8,128)(2,1)} %get-tuple-element.30), channel_id=1, source_target_pairs={{1,0},{2,1},{3,2},{5,4},{6,5},{7,6},{9,8},{10,9},{11,10},{13,12},{... | collective-permute-start | bytes 1572872 | tf_op jit(solution)/shard_map/ppermute | solution.py:35
  35.4 3.6 %maximum_select_fusion = bf16[2,9,384,128]{3,2,1,0:T(8,128)(2,1)} fusion(bf16[1,9,384,128]{3,2,1,0:T(8,128)(2,1)} %collective-permute-done.3, bf16[1,9,384,128]{3,2,1,0:T(8,128)(2,1)} %param.3, pred[]{:T(512)S(6)} %eq.3), kind=kLoop, calls=%fused_computation.47 | loop fusion | flops 2654208 | bytes 3538945 | tf_op jit(solution)/shard_map/jit(_where)/select_n | solution.py:14
  39.9 4.3 %collective-permute-done.2 = bf16[4,1,512,128]{3,2,1,0:T(8,128)(2,1)S(1)} collective-permute-done((bf16[4,1,512,128]{3,2,1,0:T(8,128)(2,1)}, bf16[4,1,512,128]{3,2,1,0:T(8,128)(2,1)S(1)}, u32[]{:S(2)}, u32[]{:S(2)}) %collective-permute-start.2) | collective-permute-done | bytes 524320 | tf_op jit(solution)/shard_map/ppermute | solution.py:35
  46.1 2.3 %fusion.50 = (bf16[4,6,512,128]{3,2,1,0:T(8,128)(2,1)S(1)}, bf16[4,6,512,128]{3,2,1,0:T(8,128)(2,1)S(1)}) fusion(bf16[4,6,514,128]{3,2,1,0:T(8,128)(2,1)S(1)} %select_maximum_fusion.3), kind=kLoop, calls=%fused_computation.89 | loop fusion | bytes 12582912 | tf_op jit(solution)/shard_map/slice | solution.py:50
  48.4 3.9 %pad_maximum_fusion = bf16[4,6,512,384]{3,2,1,0:T(8,128)(2,1)S(1)} fusion(bf16[4,6,512,128]{3,2,1,0:T(8,128)(2,1)S(1)} %get-tuple-element.26, bf16[4,1,512,128]{3,2,1,0:T(8,128)(2,1)} %copy-done.19, bf16[2,4,512,128]{3,2,1,0:T(8,128)(2,1)S(1)} %copy-done.12, bf16[2,4,512,128]{3,2,1,0:T(8,128)(2,1)S(1)} %copy-done.16, bf16[4,1,512,128]{3,2,1,0:T(8,128)(2,1)} %copy-done.18, ...), kind=kLoop, calls=%fused_computation.2 | loop fusion | flops 56623104 | bytes 18874368 | tf_op jit(solution)/shard_map/concatenate | solution.py:49
  52.4 8.4 %fusion.48 = (bf16[2,4,512,384]{3,2,1,0:T(8,128)(2,1)}, bf16[2,4,512,384]{3,2,1,0:T(8,128)(2,1)}, bf16[2,4,512,384]{3,2,1,0:T(8,128)(2,1)}, bf16[2,4,512,384]{3,...) fusion(bf16[4,6,512,384]{3,2,1,0:T(8,128)(2,1)S(1)} %pad_maximu, ...), kind=kLoop, calls=%fused_computation.87 | loop fusion | bytes 56623104 | tf_op jit(solution)/shard_map/slice | solution.py:55
  60.8 3.0 %fusion.39 = f32[4096,128]{1,0:T(8,128)S(1)} fusion(bf16[4096,384]{1,0:T(8,128)(2,1)} %bitcast.131, bf16[2,9,384,128]{3,2,1,0:T(8,128)(2,1)} %maximum_select_fusion), kind=kOutput, calls=%fused_computation.70 | convolution fusion | flops 402653184 | bytes 5341184 | tf_op jit(solution)/shard_map/dot_general | solution.py:56
  63.9 2.0 %fusion.40 = f32[4096,128]{1,0:T(8,128)S(1)} fusion(bf16[4096,384]{1,0:T(8,128)(2,1)S(1)} %bitcast.129, bf16[2,9,384,128]{3,2,1,0:T(8,128)(2,1)} %maximum_select_fusion), kind=kOutput, calls=%fused_computation.72 | convolution fusion | flops 402653184 | bytes 5341184 | tf_op jit(solution)/shard_map/dot_general | solution.py:56
  65.9 2.0 %fusion.41 = f32[4096,128]{1,0:T(8,128)S(1)} fusion(bf16[4096,384]{1,0:T(8,128)(2,1)S(1)} %bitcast.127, bf16[2,9,384,128]{3,2,1,0:T(8,128)(2,1)} %maximum_select_fusion), kind=kOutput, calls=%fused_computation.74 | convolution fusion | flops 402653184 | bytes 5341184 | tf_op jit(solution)/shard_map/dot_general | solution.py:56
  68.0 2.0 %fusion.42 = f32[4096,128]{1,0:T(8,128)S(1)} fusion(bf16[4096,384]{1,0:T(8,128)(2,1)S(1)} %bitcast.125, bf16[2,9,384,128]{3,2,1,0:T(8,128)(2,1)} %maximum_select_fusion), kind=kOutput, calls=%fused_computation.76 | convolution fusion | flops 402653184 | bytes 5341184 | tf_op jit(solution)/shard_map/dot_general | solution.py:56
  70.0 2.0 %fusion.43 = f32[4096,128]{1,0:T(8,128)S(1)} fusion(bf16[4096,384]{1,0:T(8,128)(2,1)S(1)} %bitcast.123, bf16[2,9,384,128]{3,2,1,0:T(8,128)(2,1)} %maximum_select_fusion), kind=kOutput, calls=%fused_computation.78 | convolution fusion | flops 402653184 | bytes 5341184 | tf_op jit(solution)/shard_map/dot_general | solution.py:56
  75.9 2.0 %fusion.46 = f32[4096,128]{1,0:T(8,128)S(1)} fusion(bf16[4096,384]{1,0:T(8,128)(2,1)S(1)} %bitcast.117, bf16[2,9,384,128]{3,2,1,0:T(8,128)(2,1)} %maximum_select_fusion), kind=kOutput, calls=%fused_computation.84 | convolution fusion | flops 402653184 | bytes 5341184 | tf_op jit(solution)/shard_map/dot_general | solution.py:56
  77.9 2.6 %fusion.14 = f32[4096,128]{1,0:T(8,128)S(1)} fusion(f32[4096,128]{1,0:T(8,128)S(1)} %fusion.39, f32[4096,128]{1,0:T(8,128)S(1)} %fusion.40, f32[4096,128]{1,0:T(8,128)S(1)} %fusion.41, f32[4096,128]{1,0:T(8,128)S(1)} %fusion.42, f32[4096,128]{1,0:T(8,128)S(1)} %fusion.43, f32[4096,128]{1,0:T(8,128)S(1)} %fusion.44, f32[4096,128]{1,0:T(8,128)S(1)} %fusion.45, ...), kind=kOutput, calls=%fused_computation.20 | convolution fusion | flops 406847488 | bytes 22118400 | tf_op jit(solution)/shard_map/dot_general | solution.py:56
  81.0 3.2 %collective-permute-start.4 = (bf16[2,4,512,128]{3,2,1,0:T(8,128)(2,1)S(1)}, bf16[2,4,512,128]{3,2,1,0:T(8,128)(2,1)S(1)}, u32[]{:S(2)}, u32[]{:S(2)}) collective-permute-start(bf16[2,4,512,128]{3,2,1,0:T(8,128)(2,1)S(1)} %fusion.30), channel_id=1, source_target_pairs={{0,4},{4,8},{8,12},{1,5},{5,9},{9,13},{2,6},{6,10},{10,14},{3,7},{... | collective-permute-start | bytes 3145736 | tf_op jit(solution)/shard_map/ppermute | solution.py:22
  84.3 17.3 %collective-permute-done.4 = bf16[2,4,512,128]{3,2,1,0:T(8,128)(2,1)S(1)} collective-permute-done((bf16[2,4,512,128]{3,2,1,0:T(8,128)(2,1)S(1)}, bf16[2,4,512,128]{3,2,1,0:T(8,128)(2,1)S(1)}, u32[]{:S(2)}, u32[]{:S(2)}) %collective-permute-start.4) | collective-permute-done | bytes 1048608 | tf_op jit(solution)/shard_map/ppermute | solution.py:22
  101.7 3.7 %collective-permute-start.5 = (bf16[4,1,512,128]{3,2,1,0:T(8,128)(2,1)S(1)}, bf16[4,1,512,128]{3,2,1,0:T(8,128)(2,1)S(1)}, u32[]{:S(2)}, u32[]{:S(2)}) collective-permute-start(bf16[4,1,512,128]{3,2,1,0:T(8,128)(2,1)S(1)} %get-tuple-element.27), channel_id=1, source_target_pairs={{0,1},{1,2},{2,3},{4,5},{5,6},{6,7},{8,9},{9,10},{10,11},{12,13},{... | collective-permute-start | bytes 1572872 | tf_op jit(solution)/shard_map/ppermute | solution.py:33
  105.4 1.9 %collective-permute-start.6 = (bf16[4,1,512,128]{3,2,1,0:T(8,128)(2,1)S(1)}, bf16[4,1,512,128]{3,2,1,0:T(8,128)(2,1)S(1)}, u32[]{:S(2)}, u32[]{:S(2)}) collective-permute-start(bf16[4,1,512,128]{3,2,1,0:T(8,128)(2,1)S(1)} %get-tuple-element.28), channel_id=1, source_target_pairs={{1,0},{2,1},{3,2},{5,4},{6,5},{7,6},{9,8},{10,9},{11,10},{13,12},{... | collective-permute-start | bytes 1572872 | tf_op jit(solution)/shard_map/ppermute | solution.py:35
  107.3 4.2 %collective-permute-done.5 = bf16[4,1,512,128]{3,2,1,0:T(8,128)(2,1)S(1)} collective-permute-done((bf16[4,1,512,128]{3,2,1,0:T(8,128)(2,1)S(1)}, bf16[4,1,512,128]{3,2,1,0:T(8,128)(2,1)S(1)}, u32[]{:S(2)}, u32[]{:S(2)}) %collective-permute-start.5) | collective-permute-done | bytes 524320 | tf_op jit(solution)/shard_map/ppermute | solution.py:33
  111.5 4.4 %collective-permute-done.6 = bf16[4,1,512,128]{3,2,1,0:T(8,128)(2,1)S(1)} collective-permute-done((bf16[4,1,512,128]{3,2,1,0:T(8,128)(2,1)S(1)}, bf16[4,1,512,128]{3,2,1,0:T(8,128)(2,1)S(1)}, u32[]{:S(2)}, u32[]{:S(2)}) %collective-permute-start.6) | collective-permute-done | bytes 524320 | tf_op jit(solution)/shard_map/ppermute | solution.py:35
  117.8 2.3 %fusion.49 = (bf16[4,6,512,128]{3,2,1,0:T(8,128)(2,1)S(1)}, bf16[4,6,512,128]{3,2,1,0:T(8,128)(2,1)S(1)}) fusion(bf16[4,6,514,128]{3,2,1,0:T(8,128)(2,1)S(1)} %select_maximum_fusion), kind=kLoop, calls=%fused_computation.88 | loop fusion | bytes 12582912 | tf_op jit(solution)/shard_map/slice | solution.py:50
  121.8 9.3 %fusion.47 = (bf16[2,4,512,384]{3,2,1,0:T(8,128)(2,1)}, bf16[2,4,512,384]{3,2,1,0:T(8,128)(2,1)}, bf16[2,4,512,384]{3,2,1,0:T(8,128)(2,1)}, bf16[2,4,512,384]{3,...) fusion(bf16[4,6,512,384]{3,2,1,0:T(8,128)(2,1)S(1)} %pad_maximu, ...), kind=kLoop, calls=%fused_computation.86 | loop fusion | bytes 56623104 | tf_op jit(solution)/shard_map/slice | solution.py:55
  131.2 3.0 %fusion.31 = f32[4096,128]{1,0:T(8,128)S(1)} fusion(bf16[4096,384]{1,0:T(8,128)(2,1)} %bitcast.132, bf16[2,9,384,128]{3,2,1,0:T(8,128)(2,1)} %maximum_select_fusion), kind=kOutput, calls=%fused_computation.53 | convolution fusion | flops 402653184 | bytes 5341184 | tf_op jit(solution)/shard_map/dot_general | solution.py:56
  134.2 2.0 %fusion.32 = f32[4096,128]{1,0:T(8,128)S(1)} fusion(bf16[4096,384]{1,0:T(8,128)(2,1)S(1)} %bitcast.130, bf16[2,9,384,128]{3,2,1,0:T(8,128)(2,1)} %maximum_select_fusion), kind=kOutput, calls=%fused_computation.55 | convolution fusion | flops 402653184 | bytes 5341184 | tf_op jit(solution)/shard_map/dot_general | solution.py:56
  136.2 2.0 %fusion.33 = f32[4096,128]{1,0:T(8,128)S(1)} fusion(bf16[4096,384]{1,0:T(8,128)(2,1)S(1)} %bitcast.128, bf16[2,9,384,128]{3,2,1,0:T(8,128)(2,1)} %maximum_select_fusion), kind=kOutput, calls=%fused_computation.57 | convolution fusion | flops 402653184 | bytes 5341184 | tf_op jit(solution)/shard_map/dot_general | solution.py:56
  138.3 2.0 %fusion.34 = f32[4096,128]{1,0:T(8,128)S(1)} fusion(bf16[4096,384]{1,0:T(8,128)(2,1)S(1)} %bitcast.126, bf16[2,9,384,128]{3,2,1,0:T(8,128)(2,1)} %maximum_select_fusion), kind=kOutput, calls=%fused_computation.59 | convolution fusion | flops 402653184 | bytes 5341184 | tf_op jit(solution)/shard_map/dot_general | solution.py:56
  140.3 2.0 %fusion.35 = f32[4096,128]{1,0:T(8,128)S(1)} fusion(bf16[4096,384]{1,0:T(8,128)(2,1)S(1)} %bitcast.124, bf16[2,9,384,128]{3,2,1,0:T(8,128)(2,1)} %maximum_select_fusion), kind=kOutput, calls=%fused_computation.61 | convolution fusion | flops 402653184 | bytes 5341184 | tf_op jit(solution)/shard_map/dot_general | solution.py:56
  142.4 2.0 %fusion.36 = f32[4096,128]{1,0:T(8,128)S(1)} fusion(bf16[4096,384]{1,0:T(8,128)(2,1)S(1)} %bitcast.122, bf16[2,9,384,128]{3,2,1,0:T(8,128)(2,1)} %maximum_select_fusion), kind=kOutput, calls=%fused_computation.63 | convolution fusion | flops 402653184 | bytes 5341184 | tf_op jit(solution)/shard_map/dot_general | solution.py:56
  146.3 2.0 %fusion.38 = f32[4096,128]{1,0:T(8,128)S(1)} fusion(bf16[4096,384]{1,0:T(8,128)(2,1)S(1)} %bitcast.118, bf16[2,9,384,128]{3,2,1,0:T(8,128)(2,1)} %maximum_select_fusion), kind=kOutput, calls=%fused_computation.67 | convolution fusion | flops 402653184 | bytes 5341184 | tf_op jit(solution)/shard_map/dot_general | solution.py:56
  148.4 2.5 %fusion.11 = f32[4096,128]{1,0:T(8,128)S(1)} fusion(f32[4096,128]{1,0:T(8,128)S(1)} %fusion.31, f32[4096,128]{1,0:T(8,128)S(1)} %fusion.32, f32[4096,128]{1,0:T(8,128)S(1)} %fusion.33, f32[4096,128]{1,0:T(8,128)S(1)} %fusion.34, f32[4096,128]{1,0:T(8,128)S(1)} %fusion.35, f32[4096,128]{1,0:T(8,128)S(1)} %fusion.36, f32[4096,128]{1,0:T(8,128)S(1)} %fusion.37, ...), kind=kOutput, calls=%fused_computation.17 | convolution fusion | flops 406847488 | bytes 22118400 | tf_op jit(solution)/shard_map/dot_general | solution.py:56
  (54 shorter events, 18.2 us)
Async XLA Ops:
  1.8 42.4 %copy-start.11 = (bf16[2,4,512,128]{3,2,1,0:T(8,128)(2,1)}, bf16[2,4,512,128]{3,2,1,0:T(8,128)(2,1)S(1)}, u32[]{:S(2)}) copy-start(bf16[2,4,512,128]{3,2,1,0:T(8,128)(2,1)S(1)} %fusion.24) | copy-start | bytes 3145732
  1.8 25.9 %collective-permute-start = (bf16[2,4,512,128]{3,2,1,0:T(8,128)(2,1)S(1)}, bf16[2,4,512,128]{3,2,1,0:T(8,128)(2,1)S(1)}, u32[]{:S(2)}, u32[]{:S(2)}) collective-permute-start(bf16[2,4,512,128]{3,2,1,0:T(8,128)(2,1)S(1)} %fusion.24), channel_id=1, source_target_pairs={{0,4},{4,8},{8,12},{1,5},{5,9},{9,13},{2,6},{6,10},{10,14},{3,7},{... | collective-permute-start | bytes 3145736 | tf_op jit(solution)/shard_map/ppermute | solution.py:22
  5.0 30.4 %collective-permute-start.3 = (bf16[1,9,384,128]{3,2,1,0:T(8,128)(2,1)}, bf16[1,9,384,128]{3,2,1,0:T(8,128)(2,1)}, u32[]{:S(2)}, u32[]{:S(2)}) collective-permute-start(bf16[1,9,384,128]{3,2,1,0:T(8,128)(2,1)} %param.3), channel_id=1, source_target_pairs={{0,16},{16,0},{1,17},{17,1},{2,18},{18,2},{3,19},{19,3},{4,20},{20... | collective-permute-start | bytes 2654216 | tf_op jit(solution)/shard_map/ppermute | solution.py:11
  27.7 16.5 %copy-start.15 = (bf16[2,4,512,128]{3,2,1,0:T(8,128)(2,1)}, bf16[2,4,512,128]{3,2,1,0:T(8,128)(2,1)S(1)}, u32[]{:S(2)}) copy-start(bf16[2,4,512,128]{3,2,1,0:T(8,128)(2,1)S(1)} %collective-permute-done) | copy-start | bytes 3145732
  28.9 11.0 %collective-permute-start.1 = (bf16[4,1,512,128]{3,2,1,0:T(8,128)(2,1)}, bf16[4,1,512,128]{3,2,1,0:T(8,128)(2,1)S(1)}, u32[]{:S(2)}, u32[]{:S(2)}) collective-permute-start(bf16[4,1,512,128]{3,2,1,0:T(8,128)(2,1)} %get-tuple-element.29), channel_id=1, source_target_pairs={{0,1},{1,2},{2,3},{4,5},{5,6},{6,7},{8,9},{9,10},{10,11},{12,13},{... | collective-permute-start | bytes 1572872 | tf_op jit(solution)/shard_map/ppermute | solution.py:33
  33.5 10.7 %collective-permute-start.2 = (bf16[4,1,512,128]{3,2,1,0:T(8,128)(2,1)}, bf16[4,1,512,128]{3,2,1,0:T(8,128)(2,1)S(1)}, u32[]{:S(2)}, u32[]{:S(2)}) collective-permute-start(bf16[4,1,512,128]{3,2,1,0:T(8,128)(2,1)} %get-tuple-element.30), channel_id=1, source_target_pairs={{1,0},{2,1},{3,2},{5,4},{6,5},{7,6},{9,8},{10,9},{11,10},{13,12},{... | collective-permute-start | bytes 1572872 | tf_op jit(solution)/shard_map/ppermute | solution.py:35
  39.9 6.2 %copy-start.18 = (bf16[4,1,512,128]{3,2,1,0:T(8,128)(2,1)}, bf16[4,1,512,128]{3,2,1,0:T(8,128)(2,1)S(1)}, u32[]{:S(2)}) copy-start(bf16[4,1,512,128]{3,2,1,0:T(8,128)(2,1)S(1)} %collective-permute-done.1) | copy-start | bytes 1572868
  44.2 1.9 %copy-start.19 = (bf16[4,1,512,128]{3,2,1,0:T(8,128)(2,1)}, bf16[4,1,512,128]{3,2,1,0:T(8,128)(2,1)S(1)}, u32[]{:S(2)}) copy-start(bf16[4,1,512,128]{3,2,1,0:T(8,128)(2,1)S(1)} %collective-permute-done.2) | copy-start | bytes 1572868
  46.1 2.3 %copy-start.12 = (bf16[2,4,512,128]{3,2,1,0:T(8,128)(2,1)S(1)}, bf16[2,4,512,128]{3,2,1,0:T(8,128)(2,1)}, u32[]{:S(2)}) copy-start(bf16[2,4,512,128]{3,2,1,0:T(8,128)(2,1)} %copy-done.11) | copy-start | bytes 3145732
  46.1 2.3 %copy-start.16 = (bf16[2,4,512,128]{3,2,1,0:T(8,128)(2,1)S(1)}, bf16[2,4,512,128]{3,2,1,0:T(8,128)(2,1)}, u32[]{:S(2)}) copy-start(bf16[2,4,512,128]{3,2,1,0:T(8,128)(2,1)} %copy-done.15) | copy-start | bytes 3145732
  60.8 3.0 %copy-start.9 = (bf16[2,4,512,384]{3,2,1,0:T(8,128)(2,1)S(1)}, bf16[2,4,512,384]{3,2,1,0:T(8,128)(2,1)}, u32[]{:S(2)}) copy-start(bf16[2,4,512,384]{3,2,1,0:T(8,128)(2,1)} %get-tuple-element.16) | copy-start | bytes 9437188
  63.9 2.0 %copy-start.7 = (bf16[2,4,512,384]{3,2,1,0:T(8,128)(2,1)S(1)}, bf16[2,4,512,384]{3,2,1,0:T(8,128)(2,1)}, u32[]{:S(2)}) copy-start(bf16[2,4,512,384]{3,2,1,0:T(8,128)(2,1)} %get-tuple-element.17) | copy-start | bytes 9437188
  65.9 2.0 %copy-start.5 = (bf16[2,4,512,384]{3,2,1,0:T(8,128)(2,1)S(1)}, bf16[2,4,512,384]{3,2,1,0:T(8,128)(2,1)}, u32[]{:S(2)}) copy-start(bf16[2,4,512,384]{3,2,1,0:T(8,128)(2,1)} %get-tuple-element.18) | copy-start | bytes 9437188
  68.0 2.0 %copy-start.3 = (bf16[2,4,512,384]{3,2,1,0:T(8,128)(2,1)S(1)}, bf16[2,4,512,384]{3,2,1,0:T(8,128)(2,1)}, u32[]{:S(2)}) copy-start(bf16[2,4,512,384]{3,2,1,0:T(8,128)(2,1)} %get-tuple-element.19) | copy-start | bytes 9437188
  70.0 2.0 %copy-start.1 = (bf16[2,4,512,384]{3,2,1,0:T(8,128)(2,1)S(1)}, bf16[2,4,512,384]{3,2,1,0:T(8,128)(2,1)}, u32[]{:S(2)}) copy-start(bf16[2,4,512,384]{3,2,1,0:T(8,128)(2,1)} %get-tuple-element.20) | copy-start | bytes 9437188
  75.8 2.0 %copy-start.14 = (bf16[2,4,512,384]{3,2,1,0:T(8,128)(2,1)S(1)}, bf16[2,4,512,384]{3,2,1,0:T(8,128)(2,1)}, u32[]{:S(2)}) copy-start(bf16[2,4,512,384]{3,2,1,0:T(8,128)(2,1)} %get-tuple-element.14) | copy-start | bytes 9437188
  77.9 2.6 %copy-start.17 = (bf16[1,2,4,512,128]{4,3,2,1,0:T(8,128)(2,1)S(1)}, bf16[1,2,4,512,128]{4,3,2,1,0:T(8,128)(2,1)}, u32[]{:S(2)}) copy-start(bf16[1,2,4,512,128]{4,3,2,1,0:T(8,128)(2,1)} %param.2) | copy-start | bytes 3145732
  81.0 20.6 %collective-permute-start.4 = (bf16[2,4,512,128]{3,2,1,0:T(8,128)(2,1)S(1)}, bf16[2,4,512,128]{3,2,1,0:T(8,128)(2,1)S(1)}, u32[]{:S(2)}, u32[]{:S(2)}) collective-permute-start(bf16[2,4,512,128]{3,2,1,0:T(8,128)(2,1)S(1)} %fusion.30), channel_id=1, source_target_pairs={{0,4},{4,8},{8,12},{1,5},{5,9},{9,13},{2,6},{6,10},{10,14},{3,7},{... | collective-permute-start | bytes 3145736 | tf_op jit(solution)/shard_map/ppermute | solution.py:22
  101.7 9.8 %collective-permute-start.5 = (bf16[4,1,512,128]{3,2,1,0:T(8,128)(2,1)S(1)}, bf16[4,1,512,128]{3,2,1,0:T(8,128)(2,1)S(1)}, u32[]{:S(2)}, u32[]{:S(2)}) collective-permute-start(bf16[4,1,512,128]{3,2,1,0:T(8,128)(2,1)S(1)} %get-tuple-element.27), channel_id=1, source_target_pairs={{0,1},{1,2},{2,3},{4,5},{5,6},{6,7},{8,9},{9,10},{10,11},{12,13},{... | collective-permute-start | bytes 1572872 | tf_op jit(solution)/shard_map/ppermute | solution.py:33
  105.4 10.5 %collective-permute-start.6 = (bf16[4,1,512,128]{3,2,1,0:T(8,128)(2,1)S(1)}, bf16[4,1,512,128]{3,2,1,0:T(8,128)(2,1)S(1)}, u32[]{:S(2)}, u32[]{:S(2)}) collective-permute-start(bf16[4,1,512,128]{3,2,1,0:T(8,128)(2,1)S(1)} %get-tuple-element.28), channel_id=1, source_target_pairs={{1,0},{2,1},{3,2},{5,4},{6,5},{7,6},{9,8},{10,9},{11,10},{13,12},{... | collective-permute-start | bytes 1572872 | tf_op jit(solution)/shard_map/ppermute | solution.py:35
  131.2 3.0 %copy-start.10 = (bf16[2,4,512,384]{3,2,1,0:T(8,128)(2,1)S(1)}, bf16[2,4,512,384]{3,2,1,0:T(8,128)(2,1)}, u32[]{:S(2)}) copy-start(bf16[2,4,512,384]{3,2,1,0:T(8,128)(2,1)} %get-tuple-element.7) | copy-start | bytes 9437188
  134.2 2.0 %copy-start.8 = (bf16[2,4,512,384]{3,2,1,0:T(8,128)(2,1)S(1)}, bf16[2,4,512,384]{3,2,1,0:T(8,128)(2,1)}, u32[]{:S(2)}) copy-start(bf16[2,4,512,384]{3,2,1,0:T(8,128)(2,1)} %get-tuple-element.8) | copy-start | bytes 9437188
  136.2 2.0 %copy-start.6 = (bf16[2,4,512,384]{3,2,1,0:T(8,128)(2,1)S(1)}, bf16[2,4,512,384]{3,2,1,0:T(8,128)(2,1)}, u32[]{:S(2)}) copy-start(bf16[2,4,512,384]{3,2,1,0:T(8,128)(2,1)} %get-tuple-element.9) | copy-start | bytes 9437188
  138.3 2.0 %copy-start.4 = (bf16[2,4,512,384]{3,2,1,0:T(8,128)(2,1)S(1)}, bf16[2,4,512,384]{3,2,1,0:T(8,128)(2,1)}, u32[]{:S(2)}) copy-start(bf16[2,4,512,384]{3,2,1,0:T(8,128)(2,1)} %get-tuple-element.10) | copy-start | bytes 9437188
  140.3 2.0 %copy-start.2 = (bf16[2,4,512,384]{3,2,1,0:T(8,128)(2,1)S(1)}, bf16[2,4,512,384]{3,2,1,0:T(8,128)(2,1)}, u32[]{:S(2)}) copy-start(bf16[2,4,512,384]{3,2,1,0:T(8,128)(2,1)} %get-tuple-element.11) | copy-start | bytes 9437188
  142.4 2.0 %copy-start = (bf16[2,4,512,384]{3,2,1,0:T(8,128)(2,1)S(1)}, bf16[2,4,512,384]{3,2,1,0:T(8,128)(2,1)}, u32[]{:S(2)}) copy-start(bf16[2,4,512,384]{3,2,1,0:T(8,128)(2,1)} %get-tuple-element.12) | copy-start | bytes 9437188
  146.3 2.1 %copy-start.13 = (bf16[2,4,512,384]{3,2,1,0:T(8,128)(2,1)S(1)}, bf16[2,4,512,384]{3,2,1,0:T(8,128)(2,1)}, u32[]{:S(2)}) copy-start(bf16[2,4,512,384]{3,2,1,0:T(8,128)(2,1)} %get-tuple-element.5) | copy-start | bytes 9437188
